TPU v7x, 32 devices: a whole 2x2x4 slice. The times are simulated.
32 devices in a mesh: ctx: 8 (over y, x, core), dp: 4 (over z).
Axes of the slice: x: 2, y: 2, z: 4, core: 2. Of those that a mesh axis runs over, the one named last changes fastest.
Arguments:
- tokens: bfloat16 [4, 1024, 4096], P('dp', 'ctx'), may hold values from -64 to 64
- query_weight: bfloat16 [4096, 4096], P('dp', 'ctx'), may hold values from -0.09375 to 0.09375
- keyval_matrix: bfloat16 [4096, 1024], P('dp', 'ctx'), may hold values from -0.09375 to 0.09375
- grad_out: bfloat16 [4, 1024, 4096], P('dp', 'ctx'), may hold values from -6 to 6
- blocks: int32 [4, 8, 8], replicated, may hold values from 0 to 7, as said below
- counts: int32 [4, 8], replicated, may hold values from 4 to 8, as said below
Outputs:
- attended: bfloat16 [4, 1024, 4096], P('dp', 'ctx')
- grad_query_weight: float32 [4096, 4096], P('dp', 'ctx')
- grad_keyval_weight: float32 [4096, 1024], P('dp', 'ctx')
Inputs may be any that keep to these rules, and one draw needn't show every extreme that they name: For key head g and query block i, the first counts[g, i] entries of blocks[g, i] are distinct; they are the blocks i - 1, i, i + 1, 0 and 7 that exist, then random others. Entries from counts[g, i] on are block numbers that are not attended. counts[g, i] is the number of distinct blocks among i - 1, i, i + 1, 0 and 7 that exist, plus 1 to 3.
All inputs are finite; a program needn't handle non-finite values.
Results may differ from a plain program's by a relative error of at most 0.004.
The roundings to bfloat16 on the way count: a program that leaves them out, or rounds other values in their place, can miss the bound.
Values may be sent and summed in bfloat16 or wider, within the bound.
No kernel may reach another device: no remote copies, remote signals or barrier semaphores. Data moves between devices by JAX's collectives and lax.ppermute only.
A program may use at most 128 MiB of HBM per device.

v0:
```python
import jax
import jax.numpy as jnp
from jax import lax
from jax.sharding import PartitionSpec as P


def partner(block, axis, distance):
    count = lax.axis_size(axis)
    route = []
    for low in range(count):
        high = low | 1 << distance
        if high != low and high < count:
            route += [(low, high), (high, low)]
    return lax.ppermute(block, axis, route)


def attend_part(query_rows, key_rows, vals, dout, valid, scale):
    scores = (
        jnp.einsum("nqhd,nkcd->nhqkc", query_rows, key_rows, preferred_element_type=jnp.float32)
        * scale
    )
    scores = jnp.where(valid[:, None, None, :, None], scores, -jnp.inf)
    peak = jnp.max(scores, axis=(3, 4), keepdims=True)
    expo = jnp.exp(scores - peak)
    probs = expo / jnp.sum(expo, axis=(3, 4), keepdims=True)
    probs_b = probs.astype(jnp.bfloat16)
    out = jnp.einsum("nhqkc,nkcd->nqhd", probs_b, vals, preferred_element_type=jnp.float32).astype(
        jnp.bfloat16
    )
    delta = jnp.transpose(
        jnp.sum(dout.astype(jnp.float32) * out.astype(jnp.float32), axis=3), (0, 2, 1)
    )
    dprob = jnp.einsum("nqhd,nkcd->nhqkc", dout, vals, preferred_element_type=jnp.float32)
    dscore = (probs * (dprob - delta[:, :, :, None, None]) * scale).astype(jnp.bfloat16)
    dquery = jnp.einsum(
        "nhqkc,nkcd->nqhd", dscore, key_rows, preferred_element_type=jnp.float32
    ).astype(jnp.bfloat16)
    dkeys = jnp.einsum("nhqkc,nqhd->nkcd", dscore, query_rows, preferred_element_type=jnp.float32)
    dvals = jnp.einsum("nhqkc,nqhd->nkcd", probs_b, dout, preferred_element_type=jnp.float32)
    return (out, dquery, dkeys, dvals)


def attention(q_heads, keyval_rows, dout_heads, blk, cnt):
    length = q_heads.shape[0]
    head_size = keyval_rows.shape[1] // 2
    heads = q_heads.shape[1] // head_size
    nblocks, kslots = blk.shape
    block = length // nblocks
    scale = head_size ** (-0.5)
    step = 4
    groups = nblocks // step
    key_rows = keyval_rows[:, :head_size].reshape(nblocks, block, head_size)
    vals = keyval_rows[:, head_size:].reshape(nblocks, block, head_size)
    valid = lax.broadcasted_iota(jnp.int32, (nblocks, kslots), 1) < cnt[:, None]
    query_rows = q_heads.reshape(groups, step, block, heads, head_size)
    dout = dout_heads.reshape(groups, step, block, heads, head_size)

    def one_step(args):
        q_part, d_part, b_part, v_part = args
        return attend_part(q_part, key_rows[b_part], vals[b_part], d_part, v_part, scale)

    out, dquery, dkeys, dvals = lax.map(
        one_step,
        (query_rows, dout, blk.reshape(groups, step, kslots), valid.reshape(groups, step, kslots)),
    )
    dkeys = dkeys.reshape(nblocks, kslots, block, head_size)
    dvals = dvals.reshape(nblocks, kslots, block, head_size)
    onehot = (
        (blk[None, :, :] == lax.broadcasted_iota(jnp.int32, (nblocks, 1, 1), 0)) & valid[None]
    ).astype(jnp.float32)
    key_grad = jnp.einsum("bnk,nkcd->bcd", onehot, dkeys, precision=lax.Precision.HIGHEST)
    val_grad = jnp.einsum("bnk,nkcd->bcd", onehot, dvals, precision=lax.Precision.HIGHEST)
    keyval_grad = jnp.concatenate(
        [key_grad.reshape(length, head_size), val_grad.reshape(length, head_size)], axis=1
    )
    return (
        out.reshape(length, heads * head_size),
        dquery.reshape(length, heads * head_size),
        keyval_grad,
    )


def shards(tokens, query_weight, keyval_matrix, grad_out, blocks, counts):
    local_rows = tokens[0]
    group_size = lax.axis_size("ctx") // blocks.shape[0]
    group_bits = group_size.bit_length() - 1
    device = lax.axis_index("ctx")
    query_cols = query_weight.shape[1]
    query_full, keyval_part = (
        lax.all_gather(query_weight, "dp", axis=0, tiled=True),
        lax.all_gather(keyval_matrix, "dp", axis=0, tiled=True),
    )
    all_rows = lax.all_gather(local_rows, "ctx", axis=0, tiled=True)
    keyval_cols = keyval_part
    for bit in range(group_bits):
        other = partner(keyval_cols, "ctx", bit)
        upper = device >> bit & 1 == 1
        keyval_cols = jnp.where(
            upper,
            jnp.concatenate([other, keyval_cols], axis=1),
            jnp.concatenate([keyval_cols, other], axis=1),
        )
    projected = jnp.dot(
        all_rows,
        jnp.concatenate([query_full, keyval_cols], axis=1),
        preferred_element_type=jnp.float32,
    ).astype(jnp.bfloat16)
    q_heads = projected[:, :query_cols]
    keyval_rows = projected[:, query_cols:]
    dout_heads = lax.all_to_all(grad_out[0], "ctx", split_axis=1, concat_axis=0, tiled=True)
    group_index = device // group_size
    blk = lax.dynamic_index_in_dim(blocks, group_index, 0, keepdims=False)
    cnt = lax.dynamic_index_in_dim(counts, group_index, 0, keepdims=False)
    out_heads, dquery, keyval_grad = attention(q_heads, keyval_rows, dout_heads, blk, cnt)
    attended = lax.all_to_all(out_heads, "ctx", split_axis=0, concat_axis=1, tiled=True)
    summed = keyval_grad
    for bit in range(group_bits):
        summed = summed + partner(summed, "ctx", bit)
    width = summed.shape[1] // group_size
    own_grad = lax.dynamic_slice_in_dim(summed, device % group_size * width, width, 1)
    own_grad = own_grad.astype(jnp.bfloat16)
    contract = (((0,), (0,)), ((), ()))
    grad_query = lax.dot_general(all_rows, dquery, contract, preferred_element_type=jnp.float32)
    grad_keyval = lax.dot_general(all_rows, own_grad, contract, preferred_element_type=jnp.float32)
    grad_query, grad_keyval = (
        lax.psum_scatter(grad_query, "dp", scatter_dimension=0, tiled=True),
        lax.psum_scatter(grad_keyval, "dp", scatter_dimension=0, tiled=True),
    )
    return (attended[None], grad_query, grad_keyval)


def solution(mesh):
    in_specs = (
        P("dp", "ctx", None),
        P("dp", "ctx"),
        P("dp", "ctx"),
        P("dp", "ctx", None),
        P(),
        P(),
    )
    out_specs = (P("dp", "ctx", None), P("dp", "ctx"), P("dp", "ctx"))
    return jax.shard_map(shards, mesh=mesh, in_specs=in_specs, out_specs=out_specs, check_vma=False)
```

profile of v0, /device:TPU:0, one launch (start us, length us, event | category | flops | bytes accessed | tf_op | source)
XLA Modules:
  0.0 476.1 jit_solution(6639766574015722503)
XLA Ops:
  9.4 30.8 %all-gather.7.cloned.1.call-done = bf16[4096,128]{1,0:T(8,128)(2,1)} async-done(((bf16[1024,128]{1,0:T(8,128)(2,1)}), bf16[4096,128]{1,0:T(8,128)(2,1)}) %all-gather.7.cloned.1.call-update) | async-done | bytes 1048592 | tf_op jit(solution)/shard_map/all_gather | solution.py:91
  40.3 2.3 copy.111
  42.5 4.2 all-to-all-start
  49.0 3.1 maximum_select_fusion
  52.1 70.0 %all-gather.5.cloned.1.call-done = bf16[4096,512]{1,0:T(8,128)(2,1)} async-done(((bf16[1024,512]{1,0:T(8,128)(2,1)}), bf16[4096,512]{1,0:T(8,128)(2,1)}) %all-gather.5.cloned.1.call-update) | async-done | bytes 4194320 | tf_op jit(solution)/shard_map/all_gather | solution.py:90
  122.1 54.8 %all-gather.9.cloned.1.call-done = bf16[1,1024,4096]{2,1,0:T(8,128)(2,1)} async-done(((bf16[1,128,4096]{2,1,0:T(8,128)(2,1)}), bf16[1,1024,4096]{2,1,0:T(8,128)(2,1)}) %all-gather.9.cloned.1.call-update) | async-done | bytes 8388624 | tf_op jit(solution)/shard_map/all_gather | solution.py:93
  177.0 10.4 %fusion.56 = bf16[1024,768]{0,1:T(8,128)(2,1)S(1)} fusion(bf16[1,1024,4096]{2,1,0:T(8,128)(2,1)} %all-gather.9.cloned.1.call-done, bf16[4096,256]{1,0:T(8,128)(2,1)S(1)} %maximum_select_fusion, bf16[4096,512]{1,0:T(8,128)(2,1)} %all-gather.5.cloned.1.call-done), kind=kOutput, calls=%fused_computation.57 | convolution fusion | flops 6455820288 | bytes 16252928 | tf_op jit(solution)/shard_map/dot_general | solution.py:103
  187.8 1.5 reshape.109
  189.4 65.5 %while.16 = (s32[]{:T(128)}, bf16[2,4,128,4,128]{2,4,3,1,0:T(8,128)(2,1)}, bf16[2,4,128,4,128]{4,3,2,1,0:T(4,128)(2,1)}, f32[2,4,8,128,128]{4,3,2,1,0:T(8,128)},...) while((s32[]{:T(128)}, ...), condition=%wide.region_4.5_spmd, body=%wide.region_0.4_spmd.sunk | while | flops 3275222016 | bytes 218726320 | solution.py:62
  189.7 0.7 gather_fusion.1
  190.5 1.2 constant_dynamic-slice_fusion.5
  192.1 1.3 bitcast_reduce_fusion.2
  193.4 1.8 fusion.119
  195.2 3.4 copy-done.6
  198.6 3.2 bitcast_dynamic-update-slice_fusion.8
  201.8 2.0 copy-done.7
  204.6 6.5 %bitcast_dynamic-update-slice_fusion.6 = (bf16[2,4,128,4,128]{2,4,3,1,0:T(8,128)(2,1)}, bf16[4,128,4,128]{3,1,2,0:T(8,128)(2,1)S(1)}) fusion(bf16[2,4,128,4,128]{2,4,3,1,0:T(8,128)(2,1)} %get-tuple-element.241, s32[]{:T(128)} %get-tuple-element.240, bf16[4,8,128,128,1]{3,2,4,1,0:T(8,128)(2,1)S(1)} %bitcast.231, f32[4,4,128]{2,1,0:T(4,128)S(1)} %fusion.119, ...), kind=kOutput, calls=%fused_computation.26.clone.1 | convolution fusion | flops 547618816 | bytes 10502688 | tf_op jit(solution)/shard_map/while/body/eval_jaxpr/nhqkc,nkcd->nqhd/dot_general | solution.py:27
  211.1 1.2 multiply_reduce_fusion.2
  212.3 4.3 fusion.120
  216.7 1.3 bitcast_dynamic-update-slice_fusion.7
  218.0 1.9 copy-done.5
  219.9 0.8 fusion.121
  221.3 1.0 copy-done.10
  223.1 1.2 constant_dynamic-slice_fusion.5
  224.7 1.3 bitcast_reduce_fusion.2
  226.0 1.8 fusion.119
  227.9 3.4 copy-done.6
  231.2 3.2 bitcast_dynamic-update-slice_fusion.8
  234.5 2.0 copy-done.7
  237.2 6.5 %bitcast_dynamic-update-slice_fusion.6 = (bf16[2,4,128,4,128]{2,4,3,1,0:T(8,128)(2,1)}, bf16[4,128,4,128]{3,1,2,0:T(8,128)(2,1)S(1)}) fusion(bf16[2,4,128,4,128]{2,4,3,1,0:T(8,128)(2,1)} %get-tuple-element.241, s32[]{:T(128)} %get-tuple-element.240, bf16[4,8,128,128,1]{3,2,4,1,0:T(8,128)(2,1)S(1)} %bitcast.231, f32[4,4,128]{2,1,0:T(4,128)S(1)} %fusion.119, ...), kind=kOutput, calls=%fused_computation.26.clone.1 | convolution fusion | flops 547618816 | bytes 10502688 | tf_op jit(solution)/shard_map/while/body/eval_jaxpr/nhqkc,nkcd->nqhd/dot_general | solution.py:27
  243.7 1.2 multiply_reduce_fusion.2
  245.0 4.3 fusion.120
  249.3 1.3 bitcast_dynamic-update-slice_fusion.7
  250.6 1.9 copy-done.5
  252.5 0.8 fusion.121
  253.9 1.0 copy-done.10
  254.9 7.2 %fusion.61 = f32[8,128,128]{2,0,1:T(8,128)S(1)} fusion(f32[8,8,128,128]{3,2,1,0:T(8,128)} %bitcast.237, s32[8,8]{0,1:T(8,128)S(1)} %copy-done.13, pred[8,8]{0,1:T(8,128)(4,1)S(1)} %copy-done.14), kind=kOutput, calls=%fused_computation.61 | convolution fusion | flops 100664320 | bytes 4718912 | tf_op jit(solution)/shard_map/bnk,nkcd->bcd/dot_general | solution.py:71
  262.3 5.0 %fusion.64 = f32[8,128,128]{2,0,1:T(8,128)S(1)} fusion(f32[8,8,128,128]{3,2,1,0:T(8,128)S(1)} %bitcast.238, s32[8,8]{0,1:T(8,128)S(1)} %copy-done.13, pred[8,8]{0,1:T(8,128)(4,1)S(1)} %copy-done.14), kind=kOutput, calls=%fused_computation.62 | convolution fusion | flops 100664320 | bytes 4718912 | tf_op jit(solution)/shard_map/bnk,nkcd->bcd/dot_general | solution.py:72
  267.8 2.5 collective-permute-done.1
  270.3 6.2 %fusion.44 = f32[4096,128]{0,1:T(8,128)} fusion(bf16[1,1024,4096]{2,1,0:T(8,128)(2,1)} %all-gather.9.cloned.1.call-done, s32[]{:T(128)S(6)} %select_n.51, f32[1024,128]{1,0:T(8,128)S(1)} %bitcast.234, f32[1024,128]{1,0:T(8,128)S(1)} %bitcast.236, f32[1024,256]{1,0:T(8,128)} %collective-permute-done.1), kind=kOutput, calls=%fused_computation.50 | convolution fusion | flops 1074135040 | bytes 12058628 | tf_op jit(solution)/shard_map/dot_general | solution.py:124
  276.6 10.4 %fusion.38 = f32[4096,512]{0,1:T(8,128)} fusion(bf16[1,1024,4096]{2,1,0:T(8,128)(2,1)} %all-gather.9.cloned.1.call-done, bf16[128,8,4,128]{3,2,1,0:T(4,128)(2,1)S(1)} %bitcast.240), kind=kOutput, calls=%fused_computation.46 | convolution fusion | flops 4294967296 | bytes 17825792 | tf_op jit(solution)/shard_map/dot_general | solution.py:123
  287.0 1.2 copy-done.12
  288.7 17.9 %all_to_all.32 = bf16[8,128,512]{2,1,0:T(8,128)(2,1)S(1)} all-to-all(bf16[8,128,512]{2,1,0:T(8,128)(2,1)S(1)} %copy.112), channel_id=1, replica_groups=mesh['ctx'=8,'dp'=4] {'ctx'}, dimensions={0} | all-to-all | bytes 2097152 | tf_op jit(solution)/shard_map/all_to_all | solution.py:115
  307.3 1.3 copy.81
  308.6 11.9 %reduce-scatter.5.cloned.1.call-done = f32[1024,128]{0,1:T(8,128)} async-done(((f32[4096,128]{0,1:T(8,128)}), f32[1024,128]{0,1:T(8,128)}) %reduce-scatter.5.cloned.1.call-update) | async-done | bytes 524304 | tf_op jit(solution)/shard_map/reduce_scatter | solution.py:127
  320.5 2.0 copy.83
  322.6 144.1 %reduce-scatter.3.cloned.1.call-done = f32[1024,512]{0,1:T(8,128)} async-done(((f32[4096,512]{0,1:T(8,128)}), f32[1024,512]{0,1:T(8,128)}) %reduce-scatter.3.cloned.1.call-update) | async-done | bytes 2097168 | tf_op jit(solution)/shard_map/reduce_scatter | solution.py:126
  466.7 2.9 copy.82
  (88 shorter events, 11.0 us)
Async XLA Ops:
  7.2 40.5 %copy-start = (s32[4,8,8]{2,1,0:T(8,128)S(1)}, s32[4,8,8]{2,1,0:T(8,128)}, u32[]{:S(2)}) copy-start(s32[4,8,8]{2,1,0:T(8,128)} %param.12) | copy-start | bytes 3076
  7.2 33.1 %all-gather.7.cloned.1.call-start = ((), (), s32[]{:S(2)}) async-start(), calls=%async_computation.5 | async-start | bytes 1310720 | tf_op jit(solution)/shard_map/all_gather | solution.py:91
  7.9 114.2 %all-gather.5.cloned.1.call-start = ((), (), s32[]{:S(2)}) async-start(), calls=%async_computation.4 | async-start | bytes 5242880 | tf_op jit(solution)/shard_map/all_gather | solution.py:90
  8.7 168.3 %all-gather.9.cloned.1.call-start = ((), (), s32[]{:S(2)}) async-start(), calls=%async_computation.8 | async-start | bytes 9437184 | tf_op jit(solution)/shard_map/all_gather | solution.py:93
  40.2 8.8 %collective-permute-start = (bf16[4096,128]{1,0:T(8,128)(2,1)}, bf16[4096,128]{1,0:T(8,128)(2,1)}, u32[]{:S(2)}, u32[]{:S(2)}) collective-permute-start(bf16[4096,128]{1,0:T(8,128)(2,1)} %all-gather.7.cloned.1.call-done), channel_id=1, source_target_pairs={{0,4},{4,0},{8,12},{12,8},{16,20},{20,16},{24,28},{28,24},{1,5},{5... | collective-permute-start | bytes 3145736 | tf_op jit(solution)/shard_map/ppermute | solution.py:14
  42.5 146.9 %all-to-all-start = ((bf16[128,8,512]{0,2,1:T(8,128)(2,1)}), bf16[128,8,512]{0,2,1:T(8,128)(2,1)}, u32[]{:S(2)}, u32[]{:S(2)}) async-start(bf16[128,8,512]{0,2,1:T(8,128)(2,1)} %bitcast.39), calls=%async_computation | async-start | bytes 2097152 | tf_op jit(solution)/shard_map/all_to_all | solution.py:110
  46.8 273.8 %reduce-scatter.5.cloned.1.call-start = ((), (), s32[]{:S(2)}) async-start(), calls=%async_computation.7 | async-start | bytes 2621440 | tf_op jit(solution)/shard_map/reduce_scatter | solution.py:127
  189.4 65.5 %copy-start.13 = (s32[8,8]{0,1:T(8,128)S(1)}, s32[8,8]{0,1:T(8,128)}, u32[]{:S(2)}) copy-start(s32[8,8]{0,1:T(8,128)} %copy.76) | copy-start | bytes 772
  189.4 65.5 %copy-start.14 = (pred[8,8]{0,1:T(8,128)(4,1)S(1)}, pred[8,8]{0,1:T(8,128)(4,1)}, u32[]{:S(2)}) copy-start(pred[8,8]{0,1:T(8,128)(4,1)} %iota_compare_fusion.1) | copy-start | bytes 196
  193.4 8.4 %copy-start.2 = (f32[4,8,128,128,4]{3,2,4,1,0:T(8,128)}, f32[4,8,128,128,4]{3,2,4,1,0:T(8,128)S(1)}, u32[]{:S(2)}) copy-start(f32[4,8,128,128,4]{3,2,4,1,0:T(8,128)S(1)} %get-tuple-element.224) | copy-start | bytes 25165828 | tf_op jit(solution)/shard_map/while
  193.4 5.2 %copy-start.6 = (f32[2,4,8,128,128]{4,3,2,1,0:T(8,128)S(1)}, f32[2,4,8,128,128]{4,3,2,1,0:T(8,128)}, u32[]{:S(2)}) copy-start(f32[2,4,8,128,128]{4,3,2,1,0:T(8,128)} %get-tuple-element.244) | copy-start | bytes 12582916 | tf_op jit(solution)/shard_map/while
  201.8 2.0 copy-start.7
  204.5 7.8 %copy-start.3 = (f32[4,8,128,128,4]{3,2,4,1,0:T(8,128)S(1)}, f32[4,8,128,128,4]{3,2,4,1,0:T(8,128)}, u32[]{:S(2)}) copy-start(f32[4,8,128,128,4]{3,2,4,1,0:T(8,128)} %copy-done.2) | copy-start | bytes 25165828 | tf_op jit(solution)/shard_map/while
  212.3 4.4 copy-start.4
  216.7 4.4 copy-start.9
  218.0 1.9 copy-start.5
  221.3 1.0 copy-start.10
  226.0 8.4 %copy-start.2 = (f32[4,8,128,128,4]{3,2,4,1,0:T(8,128)}, f32[4,8,128,128,4]{3,2,4,1,0:T(8,128)S(1)}, u32[]{:S(2)}) copy-start(f32[4,8,128,128,4]{3,2,4,1,0:T(8,128)S(1)} %get-tuple-element.224) | copy-start | bytes 25165828 | tf_op jit(solution)/shard_map/while
  226.0 5.2 %copy-start.6 = (f32[2,4,8,128,128]{4,3,2,1,0:T(8,128)S(1)}, f32[2,4,8,128,128]{4,3,2,1,0:T(8,128)}, u32[]{:S(2)}) copy-start(f32[2,4,8,128,128]{4,3,2,1,0:T(8,128)} %get-tuple-element.244) | copy-start | bytes 12582916 | tf_op jit(solution)/shard_map/while
  234.4 2.0 copy-start.7
  237.2 7.8 %copy-start.3 = (f32[4,8,128,128,4]{3,2,4,1,0:T(8,128)S(1)}, f32[4,8,128,128,4]{3,2,4,1,0:T(8,128)}, u32[]{:S(2)}) copy-start(f32[4,8,128,128,4]{3,2,4,1,0:T(8,128)} %copy-done.2) | copy-start | bytes 25165828 | tf_op jit(solution)/shard_map/while
  245.0 4.4 copy-start.4
  249.3 4.4 copy-start.9
  250.6 1.9 copy-start.5
  253.9 1.0 copy-start.10
  254.9 7.4 %copy-start.8 = (f32[2,4,8,128,128]{4,3,2,1,0:T(8,128)S(1)}, f32[2,4,8,128,128]{4,3,2,1,0:T(8,128)}, u32[]{:S(2)}) copy-start(f32[2,4,8,128,128]{4,3,2,1,0:T(8,128)} %get-tuple-element.66) | copy-start | bytes 12582916
  267.5 2.9 collective-permute-start.1
  267.8 8.8 %copy-start.11 = (bf16[2,4,128,4,128]{4,3,2,1,0:T(4,128)(2,1)S(1)}, bf16[2,4,128,4,128]{4,3,2,1,0:T(4,128)(2,1)}, u32[]{:S(2)}) copy-start(bf16[2,4,128,4,128]{4,3,2,1,0:T(4,128)(2,1)} %get-tuple-element.64) | copy-start | bytes 3145732
  276.5 190.2 %reduce-scatter.3.cloned.1.call-start = ((), (), s32[]{:S(2)}) async-start(), calls=%async_computation.6 | async-start | bytes 10485760 | tf_op jit(solution)/shard_map/reduce_scatter | solution.py:126
  287.0 1.2 copy-start.12
  288.2 181.4 %copy-start.1 = (s32[4,8,8]{2,1,0:T(8,128)S(1)}, s32[4,8,8]{2,1,0:T(8,128)}, u32[]{:S(2)}) copy-start(s32[4,8,8]{2,1,0:T(8,128)} %param.12) | copy-start | bytes 3076
Sparse Core Ops, SparseCore 0:
  9.6 30.6 all-gather.6
  41.8 80.2 all-gather.4
  124.0 52.9 all-gather.8
  276.6 43.8 reduce-scatter.4
  322.9 143.8 reduce-scatter.2
where the time goes:
time: 477 us; the launch traced here: 476 us
  waiting for transfers between devices  316 us (66%)
  matrix products  74 us (16%)
  local copies, waits for them, and re-layouts  38.6 us (8%)
  blocking collectives  17.9 us (4%)
  between operations  14 us (3%)
  other arithmetic  9.91 us (2%)
    reduce_scatter x1, waiting for transfers between devices, shards(): lax.psum_scatter(grad_query, 'dp', scatter_dimension=0, tiled=True)  144 us
    all_gather x1, waiting for transfers between devices, shards(): lax.all_gather(query_weight, 'dp', axis=0, tiled=True)  70 us
    all_gather x1, waiting for transfers between devices, shards(): all_rows = lax.all_gather(local_rows, 'ctx', axis=0, tiled=True)  54.8 us
    all_gather x1, waiting for transfers between devices, shards(): lax.all_gather(keyval_matrix, 'dp', axis=0, tiled=True)  30.8 us
    all_to_all x1, blocking collectives, shards(): lax.all_to_all(out_heads, 'ctx', split_axis=0, concat_axis=1, tiled=True)  17.9 us
    while x32, local copies, waits for them, and re-layouts  16.6 us
    dot_general x2, matrix products, attend_part(): jnp.einsum('nhqkc,nkcd->nqhd', probs_b, vals, preferred_element_type=jnp....  13.1 us
    reduce_scatter x1, waiting for transfers between devices, shards(): lax.psum_scatter(grad_keyval, 'dp', scatter_dimension=0, tiled=True)  11.9 us
  transfers between devices with their start and end apart: 8, of which 6 were waited for; matrix products, arithmetic and copies ran while one was open for 7% of the time, Pallas kernels for 0%

commit v1 on v0

--- a/solution.py
+++ b/solution.py
@@ -2,6 +2,28 @@
 import jax.numpy as jnp
 from jax import lax
 from jax.sharding import PartitionSpec as P
+
+
+def map_sector(load):
+    t_next, next_value, odd = (lax.axis_size("dp"), lax.axis_index("dp"), load.shape[0])
+    taken_in = lax.dynamic_update_slice_in_dim(
+        jnp.zeros([j * t_next if num == 0 else j for num, j in enumerate(load.shape)], load.dtype),
+        load,
+        next_value * odd,
+        axis=0,
+    )
+    row_out = small = load
+    for q in tuple(range(1, t_next // 2 + 1)):
+        row_out = lax.ppermute(row_out, "dp", [(num, (num + 1) % t_next) for num in range(t_next)])
+        taken_in = lax.dynamic_update_slice_in_dim(
+            taken_in, row_out, (next_value - q) % t_next * odd, axis=0
+        )
+        if 2 * q < t_next:
+            small = lax.ppermute(small, "dp", [(num, (num - 1) % t_next) for num in range(t_next)])
+            taken_in = lax.dynamic_update_slice_in_dim(
+                taken_in, small, (next_value + q) % t_next * odd, axis=0
+            )
+    return taken_in
 
 
 def partner(block, axis, distance):
@@ -88,7 +110,7 @@
     query_cols = query_weight.shape[1]
     query_full, keyval_part = (
         lax.all_gather(query_weight, "dp", axis=0, tiled=True),
-        lax.all_gather(keyval_matrix, "dp", axis=0, tiled=True),
+        map_sector(keyval_matrix),
     )
     all_rows = lax.all_gather(local_rows, "ctx", axis=0, tiled=True)
     keyval_cols = keyval_part

time: 477 us -> 457 us (0.958)
  waiting for transfers between devices: 316 us -> 289 us
  starting transfers between devices: 4.76 us -> 9.99 us
    all_gather x1 -> x0, waiting for transfers between devices: 30.8 us -> none  [shards(): lax.all_gather(keyval_matrix, 'dp', axis=0, tiled=True)]
    ppermute x0 -> x3, waiting for transfers between devices: none -> 23.5 us  [the longest x2 15.7 us: map_sector(): lax.ppermute(row_out, 'dp', [(num, (num + 1) % t_next) for num in range(t...]
    all_gather x1, waiting for transfers between devices: 70 us -> 50 us  [shards(): lax.all_gather(query_weight, 'dp', axis=0, tiled=True)]
    ppermute x0 -> x3, starting transfers between devices: none -> 5.17 us  [the longest x2 3.08 us: map_sector(): lax.ppermute(row_out, 'dp', [(num, (num + 1) % t_next) for num in range(t...]
  transfers between devices with their start and end apart: 8 -> 10, of which waited for: 6 -> 8; matrix products, arithmetic and copies ran while one was open for 7% -> 8% of each run, Pallas kernels for 0% -> 0%
where the time goes in v1:
time: 457 us
  waiting for transfers between devices  289 us (63%)
  matrix products  74.1 us (16%)
  local copies, waits for them, and re-layouts  42.1 us (9%)
  blocking collectives  17.9 us (4%)
  between operations  14.1 us (3%)
  starting transfers between devices  9.99 us (2%)
  other arithmetic  8.97 us (2%)
    reduce_scatter x1, waiting for transfers between devices, shards(): lax.psum_scatter(grad_query, 'dp', scatter_dimension=0, tiled=True)  144 us
    all_gather x1, waiting for transfers between devices, shards(): all_rows = lax.all_gather(local_rows, 'ctx', axis=0, tiled=True)  55.5 us
    all_gather x1, waiting for transfers between devices, shards(): lax.all_gather(query_weight, 'dp', axis=0, tiled=True)  50 us
    all_to_all x1, blocking collectives, shards(): lax.all_to_all(out_heads, 'ctx', split_axis=0, concat_axis=1, tiled=True)  17.9 us
    while x32, local copies, waits for them, and re-layouts  16.5 us
    ppermute x2, waiting for transfers between devices, map_sector(): lax.ppermute(row_out, 'dp', [(num, (num + 1) % t_next) for num in range(t...  15.7 us
    dot_general x2, matrix products, attend_part(): jnp.einsum('nhqkc,nkcd->nqhd', probs_b, vals, preferred_element_type=jnp....  13.1 us
    reduce_scatter x1, waiting for transfers between devices, shards(): lax.psum_scatter(grad_keyval, 'dp', scatter_dimension=0, tiled=True)  11.8 us
  transfers between devices with their start and end apart: 10, of which 8 were waited for; matrix products, arithmetic and copies ran while one was open for 8% of the time, Pallas kernels for 0%

profile of v1, /device:TPU:0, one launch (start us, length us, event | category | flops | bytes accessed | tf_op | source)
XLA Modules:
  0.0 456.7 jit_solution(9961825338445962620)
XLA Ops:
  8.7 3.1 collective-permute-start
  11.7 2.1 collective-permute-start.1
  13.8 7.3 %collective-permute-done = bf16[1024,128]{1,0:T(8,128)(2,1)S(1)} collective-permute-done((bf16[1024,128]{1,0:T(8,128)(2,1)}, bf16[1024,128]{1,0:T(8,128)(2,1)S(1)}, u32[]{:S(2)}, u32[]{:S(2)}) %collective-permute-start) | collective-permute-done | bytes 262176 | tf_op jit(solution)/shard_map/ppermute | solution.py:17
  22.4 7.9 %collective-permute-done.1 = bf16[1024,128]{1,0:T(8,128)(2,1)S(1)} collective-permute-done((bf16[1024,128]{1,0:T(8,128)(2,1)}, bf16[1024,128]{1,0:T(8,128)(2,1)S(1)}, u32[]{:S(2)}, u32[]{:S(2)}) %collective-permute-start.1) | collective-permute-done | bytes 262176 | tf_op jit(solution)/shard_map/ppermute | solution.py:22
  30.3 8.4 %collective-permute-done.2 = bf16[1024,128]{1,0:T(8,128)(2,1)S(1)} collective-permute-done((bf16[1024,128]{1,0:T(8,128)(2,1)S(1)}, bf16[1024,128]{1,0:T(8,128)(2,1)S(1)}, u32[]{:S(2)}, u32[]{:S(2)}) %collective-permute-start.2) | collective-permute-done | bytes 262176 | tf_op jit(solution)/shard_map/ppermute | solution.py:17
  38.8 2.3 copy.111
  41.1 4.2 all-to-all-start
  47.5 2.2 maximum_select_fusion
  49.7 50.0 %all-gather.4.cloned.1.call-done = bf16[4096,512]{1,0:T(8,128)(2,1)} async-done(((bf16[1024,512]{1,0:T(8,128)(2,1)}), bf16[4096,512]{1,0:T(8,128)(2,1)}) %all-gather.4.cloned.1.call-update) | async-done | bytes 4194320 | tf_op jit(solution)/shard_map/all_gather | solution.py:112
  99.8 55.5 %all-gather.6.cloned.1.call-done = bf16[1,1024,4096]{2,1,0:T(8,128)(2,1)} async-done(((bf16[1,128,4096]{2,1,0:T(8,128)(2,1)}), bf16[1,1024,4096]{2,1,0:T(8,128)(2,1)}) %all-gather.6.cloned.1.call-update) | async-done | bytes 8388624 | tf_op jit(solution)/shard_map/all_gather | solution.py:115
  155.2 10.4 %fusion.56 = bf16[1024,768]{0,1:T(8,128)(2,1)S(1)} fusion(bf16[1,1024,4096]{2,1,0:T(8,128)(2,1)} %all-gather.6.cloned.1.call-done, bf16[4096,256]{1,0:T(8,128)(2,1)S(1)} %maximum_select_fusion, bf16[4096,512]{1,0:T(8,128)(2,1)} %all-gather.4.cloned.1.call-done), kind=kOutput, calls=%fused_computation.57 | convolution fusion | flops 6455820288 | bytes 16252928 | tf_op jit(solution)/shard_map/dot_general | solution.py:125
  165.7 1.1 copy-done.9
  166.9 1.6 reshape.109
  169.9 65.5 %while.16 = (s32[]{:T(128)}, bf16[2,4,128,4,128]{2,4,3,1,0:T(8,128)(2,1)}, bf16[2,4,128,4,128]{4,3,2,1,0:T(4,128)(2,1)}, f32[2,4,8,128,128]{4,3,2,1,0:T(8,128)},...) while((s32[]{:T(128)}, ...), condition=%wide.region_4.5_spmd, body=%wide.region_0.4_spmd.sunk | while | flops 3275222016 | bytes 218726320 | solution.py:84
  171.0 1.2 constant_dynamic-slice_fusion.5
  172.6 1.3 bitcast_reduce_fusion.2
  173.9 1.8 fusion.119
  175.7 3.4 copy-done.6
  179.1 3.2 bitcast_dynamic-update-slice_fusion.8
  182.3 2.0 copy-done.7
  185.1 6.5 %bitcast_dynamic-update-slice_fusion.6 = (bf16[2,4,128,4,128]{2,4,3,1,0:T(8,128)(2,1)}, bf16[4,128,4,128]{3,1,2,0:T(8,128)(2,1)S(1)}) fusion(bf16[2,4,128,4,128]{2,4,3,1,0:T(8,128)(2,1)} %get-tuple-element.241, s32[]{:T(128)} %get-tuple-element.240, bf16[4,8,128,128,1]{3,2,4,1,0:T(8,128)(2,1)S(1)} %bitcast.231, f32[4,4,128]{2,1,0:T(4,128)S(1)} %fusion.119, ...), kind=kOutput, calls=%fused_computation.26.clone.1 | convolution fusion | flops 547618816 | bytes 10502688 | tf_op jit(solution)/shard_map/while/body/eval_jaxpr/nhqkc,nkcd->nqhd/dot_general | solution.py:49
  191.6 1.2 multiply_reduce_fusion.2
  192.8 4.3 fusion.120
  197.2 1.3 bitcast_dynamic-update-slice_fusion.7
  198.5 1.9 copy-done.5
  203.6 1.2 constant_dynamic-slice_fusion.5
  205.2 1.3 bitcast_reduce_fusion.2
  206.5 1.8 fusion.119
  208.4 3.4 copy-done.6
  211.8 3.2 bitcast_dynamic-update-slice_fusion.8
  215.0 2.0 copy-done.7
  217.7 6.5 %bitcast_dynamic-update-slice_fusion.6 = (bf16[2,4,128,4,128]{2,4,3,1,0:T(8,128)(2,1)}, bf16[4,128,4,128]{3,1,2,0:T(8,128)(2,1)S(1)}) fusion(bf16[2,4,128,4,128]{2,4,3,1,0:T(8,128)(2,1)} %get-tuple-element.241, s32[]{:T(128)} %get-tuple-element.240, bf16[4,8,128,128,1]{3,2,4,1,0:T(8,128)(2,1)S(1)} %bitcast.231, f32[4,4,128]{2,1,0:T(4,128)S(1)} %fusion.119, ...), kind=kOutput, calls=%fused_computation.26.clone.1 | convolution fusion | flops 547618816 | bytes 10502688 | tf_op jit(solution)/shard_map/while/body/eval_jaxpr/nhqkc,nkcd->nqhd/dot_general | solution.py:49
  224.3 1.2 multiply_reduce_fusion.2
  225.5 4.3 fusion.120
  229.9 1.3 bitcast_dynamic-update-slice_fusion.7
  231.1 1.9 copy-done.5
  235.4 7.2 %fusion.61 = f32[8,128,128]{2,0,1:T(8,128)S(1)} fusion(f32[8,8,128,128]{3,2,1,0:T(8,128)} %bitcast.237, s32[8,8]{0,1:T(8,128)S(1)} %copy-done.14, pred[8,8]{0,1:T(8,128)(4,1)S(1)} %copy-done.15), kind=kOutput, calls=%fused_computation.61 | convolution fusion | flops 100664320 | bytes 4718912 | tf_op jit(solution)/shard_map/bnk,nkcd->bcd/dot_general | solution.py:93
  242.8 5.0 %fusion.64 = f32[8,128,128]{2,0,1:T(8,128)S(1)} fusion(f32[8,8,128,128]{3,2,1,0:T(8,128)S(1)} %bitcast.238, s32[8,8]{0,1:T(8,128)S(1)} %copy-done.14, pred[8,8]{0,1:T(8,128)(4,1)S(1)} %copy-done.15), kind=kOutput, calls=%fused_computation.62 | convolution fusion | flops 100664320 | bytes 4718912 | tf_op jit(solution)/shard_map/bnk,nkcd->bcd/dot_general | solution.py:94
  248.3 2.5 collective-permute-done.4
  250.8 6.2 %fusion.44 = f32[4096,128]{0,1:T(8,128)} fusion(bf16[1,1024,4096]{2,1,0:T(8,128)(2,1)} %all-gather.6.cloned.1.call-done, s32[]{:T(128)S(6)} %select_n.82, f32[1024,128]{1,0:T(8,128)S(1)} %bitcast.234, f32[1024,128]{1,0:T(8,128)S(1)} %bitcast.236, f32[1024,256]{1,0:T(8,128)} %collective-permute-done.4), kind=kOutput, calls=%fused_computation.50 | convolution fusion | flops 1074135040 | bytes 12058628 | tf_op jit(solution)/shard_map/dot_general | solution.py:146
  257.1 10.4 %fusion.38 = f32[4096,512]{0,1:T(8,128)} fusion(bf16[1,1024,4096]{2,1,0:T(8,128)(2,1)} %all-gather.6.cloned.1.call-done, bf16[128,8,4,128]{3,2,1,0:T(4,128)(2,1)S(1)} %bitcast.240), kind=kOutput, calls=%fused_computation.46 | convolution fusion | flops 4294967296 | bytes 17825792 | tf_op jit(solution)/shard_map/dot_general | solution.py:145
  267.5 1.2 copy-done.13
  269.3 17.9 %all_to_all.32 = bf16[8,128,512]{2,1,0:T(8,128)(2,1)S(1)} all-to-all(bf16[8,128,512]{2,1,0:T(8,128)(2,1)S(1)} %copy.112), channel_id=1, replica_groups=mesh['ctx'=8,'dp'=4] {'ctx'}, dimensions={0} | all-to-all | bytes 2097152 | tf_op jit(solution)/shard_map/all_to_all | solution.py:137
  287.8 1.3 copy.81
  289.2 11.8 %reduce-scatter.5.cloned.1.call-done = f32[1024,128]{0,1:T(8,128)} async-done(((f32[4096,128]{0,1:T(8,128)}), f32[1024,128]{0,1:T(8,128)}) %reduce-scatter.5.cloned.1.call-update) | async-done | bytes 524304 | tf_op jit(solution)/shard_map/reduce_scatter | solution.py:149
  301.0 2.0 copy.83
  303.0 144.2 %reduce-scatter.3.cloned.1.call-done = f32[1024,512]{0,1:T(8,128)} async-done(((f32[4096,512]{0,1:T(8,128)}), f32[1024,512]{0,1:T(8,128)}) %reduce-scatter.3.cloned.1.call-update) | async-done | bytes 2097168 | tf_op jit(solution)/shard_map/reduce_scatter | solution.py:148
  447.2 2.9 copy.82
  (98 shorter events, 17.0 us)
Async XLA Ops:
  7.2 39.1 %copy-start = (s32[4,8,8]{2,1,0:T(8,128)S(1)}, s32[4,8,8]{2,1,0:T(8,128)}, u32[]{:S(2)}) copy-start(s32[4,8,8]{2,1,0:T(8,128)} %param.12) | copy-start | bytes 3076
  7.2 92.6 %all-gather.4.cloned.1.call-start = ((), (), s32[]{:S(2)}) async-start(), calls=%async_computation.4 | async-start | bytes 5242880 | tf_op jit(solution)/shard_map/all_gather | solution.py:112
  7.9 147.3 %all-gather.6.cloned.1.call-start = ((), (), s32[]{:S(2)}) async-start(), calls=%async_computation.7 | async-start | bytes 9437184 | tf_op jit(solution)/shard_map/all_gather | solution.py:115
  8.7 12.5 %collective-permute-start = (bf16[1024,128]{1,0:T(8,128)(2,1)}, bf16[1024,128]{1,0:T(8,128)(2,1)S(1)}, u32[]{:S(2)}, u32[]{:S(2)}) collective-permute-start(bf16[1024,128]{1,0:T(8,128)(2,1)} %param.10), channel_id=1, source_target_pairs={{0,1},{1,2},{2,3},{3,0},{4,5},{5,6},{6,7},{7,4},{8,9},{9,10},{10,1... | collective-permute-start | bytes 786440 | tf_op jit(solution)/shard_map/ppermute | solution.py:17
  11.7 18.5 %collective-permute-start.1 = (bf16[1024,128]{1,0:T(8,128)(2,1)}, bf16[1024,128]{1,0:T(8,128)(2,1)S(1)}, u32[]{:S(2)}, u32[]{:S(2)}) collective-permute-start(bf16[1024,128]{1,0:T(8,128)(2,1)} %param.10), channel_id=1, source_target_pairs={{0,3},{1,0},{2,1},{3,2},{4,7},{5,4},{6,5},{7,6},{8,11},{9,8},{10,9... | collective-permute-start | bytes 786440 | tf_op jit(solution)/shard_map/ppermute | solution.py:22
  21.2 17.5 %collective-permute-start.2 = (bf16[1024,128]{1,0:T(8,128)(2,1)S(1)}, bf16[1024,128]{1,0:T(8,128)(2,1)S(1)}, u32[]{:S(2)}, u32[]{:S(2)}) collective-permute-start(bf16[1024,128]{1,0:T(8,128)(2,1)S(1)} %collective-permute-done), channel_id=1, source_target_pairs={{0,1},{1,2},{2,3},{3,0},{4,5},{5,6},{6,7},{7,4},{8,9},{9,10},{10,1... | collective-permute-start | bytes 786440 | tf_op jit(solution)/shard_map/ppermute | solution.py:17
  38.7 8.8 %collective-permute-start.3 = (bf16[4096,128]{1,0:T(8,128)(2,1)S(1)}, bf16[4096,128]{1,0:T(8,128)(2,1)}, u32[]{:S(2)}, u32[]{:S(2)}) collective-permute-start(bf16[4096,128]{1,0:T(8,128)(2,1)S(1)} %constant_dynamic-update-slice_fusion.1), channel_id=1, source_target_pairs={{0,4},{4,0},{8,12},{12,8},{16,20},{20,16},{24,28},{28,24},{1,5},{5... | collective-permute-start | bytes 3145736 | tf_op jit(solution)/shard_map/ppermute | solution.py:36
  41.1 128.8 %all-to-all-start = ((bf16[128,8,512]{0,2,1:T(8,128)(2,1)}), bf16[128,8,512]{0,2,1:T(8,128)(2,1)}, u32[]{:S(2)}, u32[]{:S(2)}) async-start(bf16[128,8,512]{0,2,1:T(8,128)(2,1)} %bitcast.39), calls=%async_computation | async-start | bytes 2097152 | tf_op jit(solution)/shard_map/all_to_all | solution.py:132
  45.3 255.7 %reduce-scatter.5.cloned.1.call-start = ((), (), s32[]{:S(2)}) async-start(), calls=%async_computation.6 | async-start | bytes 2621440 | tf_op jit(solution)/shard_map/reduce_scatter | solution.py:149
  165.7 1.1 copy-start.9
  169.9 65.5 %copy-start.14 = (s32[8,8]{0,1:T(8,128)S(1)}, s32[8,8]{0,1:T(8,128)}, u32[]{:S(2)}) copy-start(s32[8,8]{0,1:T(8,128)} %copy.76) | copy-start | bytes 772
  169.9 65.5 %copy-start.15 = (pred[8,8]{0,1:T(8,128)(4,1)S(1)}, pred[8,8]{0,1:T(8,128)(4,1)}, u32[]{:S(2)}) copy-start(pred[8,8]{0,1:T(8,128)(4,1)} %iota_compare_fusion.1) | copy-start | bytes 196
  173.9 8.4 %copy-start.2 = (f32[4,8,128,128,4]{3,2,4,1,0:T(8,128)}, f32[4,8,128,128,4]{3,2,4,1,0:T(8,128)S(1)}, u32[]{:S(2)}) copy-start(f32[4,8,128,128,4]{3,2,4,1,0:T(8,128)S(1)} %get-tuple-element.224) | copy-start | bytes 25165828 | tf_op jit(solution)/shard_map/while
  173.9 5.2 %copy-start.6 = (f32[2,4,8,128,128]{4,3,2,1,0:T(8,128)S(1)}, f32[2,4,8,128,128]{4,3,2,1,0:T(8,128)}, u32[]{:S(2)}) copy-start(f32[2,4,8,128,128]{4,3,2,1,0:T(8,128)} %get-tuple-element.244) | copy-start | bytes 12582916 | tf_op jit(solution)/shard_map/while
  182.3 2.0 copy-start.7
  185.1 7.8 %copy-start.3 = (f32[4,8,128,128,4]{3,2,4,1,0:T(8,128)S(1)}, f32[4,8,128,128,4]{3,2,4,1,0:T(8,128)}, u32[]{:S(2)}) copy-start(f32[4,8,128,128,4]{3,2,4,1,0:T(8,128)} %copy-done.2) | copy-start | bytes 25165828 | tf_op jit(solution)/shard_map/while
  192.8 4.4 copy-start.4
  197.2 4.4 copy-start.10
  198.5 1.9 copy-start.5
  201.8 1.0 copy-start.11
  206.5 8.4 %copy-start.2 = (f32[4,8,128,128,4]{3,2,4,1,0:T(8,128)}, f32[4,8,128,128,4]{3,2,4,1,0:T(8,128)S(1)}, u32[]{:S(2)}) copy-start(f32[4,8,128,128,4]{3,2,4,1,0:T(8,128)S(1)} %get-tuple-element.224) | copy-start | bytes 25165828 | tf_op jit(solution)/shard_map/while
  206.5 5.2 %copy-start.6 = (f32[2,4,8,128,128]{4,3,2,1,0:T(8,128)S(1)}, f32[2,4,8,128,128]{4,3,2,1,0:T(8,128)}, u32[]{:S(2)}) copy-start(f32[2,4,8,128,128]{4,3,2,1,0:T(8,128)} %get-tuple-element.244) | copy-start | bytes 12582916 | tf_op jit(solution)/shard_map/while
  215.0 2.0 copy-start.7
  217.7 7.8 %copy-start.3 = (f32[4,8,128,128,4]{3,2,4,1,0:T(8,128)S(1)}, f32[4,8,128,128,4]{3,2,4,1,0:T(8,128)}, u32[]{:S(2)}) copy-start(f32[4,8,128,128,4]{3,2,4,1,0:T(8,128)} %copy-done.2) | copy-start | bytes 25165828 | tf_op jit(solution)/shard_map/while
  225.5 4.4 copy-start.4
  229.9 4.4 copy-start.10
  231.1 1.9 copy-start.5
  234.4 1.0 copy-start.11
  235.4 7.4 %copy-start.8 = (f32[2,4,8,128,128]{4,3,2,1,0:T(8,128)S(1)}, f32[2,4,8,128,128]{4,3,2,1,0:T(8,128)}, u32[]{:S(2)}) copy-start(f32[2,4,8,128,128]{4,3,2,1,0:T(8,128)} %get-tuple-element.66) | copy-start | bytes 12582916
  248.0 2.9 collective-permute-start.4
  248.3 8.8 %copy-start.12 = (bf16[2,4,128,4,128]{4,3,2,1,0:T(4,128)(2,1)S(1)}, bf16[2,4,128,4,128]{4,3,2,1,0:T(4,128)(2,1)}, u32[]{:S(2)}) copy-start(bf16[2,4,128,4,128]{4,3,2,1,0:T(4,128)(2,1)} %get-tuple-element.64) | copy-start | bytes 3145732
  257.0 190.2 %reduce-scatter.3.cloned.1.call-start = ((), (), s32[]{:S(2)}) async-start(), calls=%async_computation.5 | async-start | bytes 10485760 | tf_op jit(solution)/shard_map/reduce_scatter | solution.py:148
  267.5 1.2 copy-start.13
  268.7 181.4 %copy-start.1 = (s32[4,8,8]{2,1,0:T(8,128)S(1)}, s32[4,8,8]{2,1,0:T(8,128)}, u32[]{:S(2)}) copy-start(s32[4,8,8]{2,1,0:T(8,128)} %param.12) | copy-start | bytes 3076
Sparse Core Ops, SparseCore 0:
  9.6 90.1 all-gather.3
  101.6 53.5 all-gather.5
  257.2 43.7 reduce-scatter.4
  303.3 143.8 reduce-scatter.2
